TPU v7x, 256 devices: a whole 4x4x8 slice. The times are simulated.
256 devices in a mesh: tm: 64 (over z, x, core), wafer: 4 (over y).
Axes of the slice: x: 4, y: 4, z: 8, core: 2. Of those that a mesh axis runs over, the one named last changes fastest.
Arguments:
- timestream: bfloat16 [1024, 262144], P('wafer', 'tm'), may hold values from -6 to 6
- sample_weight: bfloat16 [1024, 262144], P('wafer', 'tm'), may hold values from 0 to 4
- response: float32 [3, 1024], replicated, may hold values from -1 to 1
- band_filter: bfloat16 [256, 256], replicated, may hold values from -0.375 to 0.375
- whiten: bfloat16 [7, 1024, 1024], P(None, ('tm', 'wafer')), as said below
- group_wafer: int32 [64], replicated, may hold values from 0 to 6
- pointing: bfloat16 [1024, 6, 256, 256], P(('tm', 'wafer')), may hold values from -0.15625 to 0.15625
- tile_list: int32 [1024, 6], P(('tm', 'wafer')), may hold values from 0 to 2047, as said below
- tile_home: int32 [2048], replicated, may hold values from 0 to 2047, as said below
- solution: float32 [2048, 3, 256], P('tm'), may hold values from -6 to 6
- direction: float32 [2048, 3, 256], P('tm'), may hold values from -6 to 6
- cg_scalars: float32 [2], replicated, may hold values from 0.5 to 1.5
Outputs:
- solution_next: float32 [2048, 3, 256], P('tm')
- residual_next: float32 [2048, 3, 256], P('tm')
- direction_next: float32 [2048, 3, 256], P('tm')
Inputs may be any that keep to these rules, and one draw needn't show every extreme that they name: `tile_list`: the tiles named in the spans of one device (one index of tm and one of wafer) are all different; among them at most 2 have their row tile_home on one index of tm, and in every draw, for each index of wafer, some index of tm owns exactly 2 tiles named by every device of that wafer index. A permutation: row tile_home[i] of a map holds sky tile i. `whiten`: each whitening matrix is symmetric.
All inputs are finite; a program needn't handle non-finite values.
Results may differ from a plain program's by a relative error of at most 0.0033.
The roundings to bfloat16 on the way count: a program that leaves them out, or rounds other values in their place, can miss the bound.
Values may be sent and summed in bfloat16 or wider, within the bound.
No kernel may reach another device: no remote copies, remote signals or barrier semaphores. Data moves between devices by JAX's collectives and lax.ppermute only.
A program may use at most 128 MiB of HBM per device.

v0:
```python
import jax
import jax.numpy as jnp
from jax import lax
from jax.sharding import PartitionSpec as P


def shards(
    timestream,
    sample_weight,
    response,
    band_filter,
    whiten,
    group_wafer,
    pointing,
    tile_list,
    tile_home,
    solution,
    direction,
    cg_scalars,
):
    precise_mode = lax.Precision.HIGHEST
    tm_count = lax.axis_size("tm")
    tm_index = lax.axis_index("tm")
    step_size = cg_scalars[0]
    blend_weight = cg_scalars[1]
    updated = solution + step_size * direction
    short_map = updated.astype(jnp.bfloat16)
    tiles_own, comp_count, pixel_count = solution.shape
    spans_here, per_span = tile_list.shape
    samples = band_filter.shape[0]
    det_total = whiten.shape[2]
    row_count = spans_here * per_span
    capacity = max(2, (row_count + tm_count - 1) // tm_count)
    tile_ids = tile_list.reshape(row_count)
    home_rows = jnp.take(tile_home, tile_ids, axis=0)
    owners = home_rows // tiles_own
    local_slot = home_rows % tiles_own
    positions = jnp.arange(row_count, dtype=jnp.int32)
    earlier = (owners[:, None] == owners[None, :]) & (positions[None, :] < positions[:, None])
    before_count = jnp.sum(earlier.astype(jnp.int32), axis=1)
    targets = owners * capacity + before_count
    placing = targets[:, None] == jnp.arange(tm_count * capacity, dtype=jnp.int32)[None, :]
    requests = jnp.sum(jnp.where(placing, local_slot[:, None], 0), axis=0)
    requests = requests.reshape(tm_count, capacity)
    asked_slots = lax.all_to_all(requests, "tm", split_axis=0, concat_axis=0, tiled=True)
    served = jnp.take(short_map, asked_slots, axis=0)
    replies, asked_slots = (
        lax.all_to_all(served, "tm", split_axis=0, concat_axis=0, tiled=True),
        asked_slots,
    )
    fetched = jnp.take(
        replies.reshape(tm_count * capacity, comp_count, pixel_count), targets, axis=0
    )
    fetched = fetched.reshape(spans_here, per_span, comp_count, pixel_count)
    signal_parts = jnp.einsum(
        "cktp,ckjp->cjt", pointing, fetched, preferred_element_type=jnp.float32
    )
    wafer_pick = group_wafer[tm_index]
    matrix = lax.dynamic_index_in_dim(
        lax.all_gather(whiten, ("tm", "wafer"), axis=1, tiled=True), wafer_pick, 0, keepdims=False
    )
    columns, column_weights = (
        lax.all_to_all(timestream, "wafer", split_axis=1, concat_axis=0, tiled=True),
        lax.all_to_all(sample_weight, "wafer", split_axis=1, concat_axis=0, tiled=True),
    )
    column_weights = column_weights.astype(jnp.float32).reshape(det_total, spans_here, samples)
    signal = jnp.einsum("jd,cjt->dct", response, signal_parts, precision=precise_mode)
    errors = (
        (columns.astype(jnp.float32).reshape(det_total, spans_here, samples) - signal)
        * column_weights
    ).astype(jnp.bfloat16)
    filtered = jnp.dot(
        errors.reshape(det_total * spans_here, samples),
        band_filter,
        preferred_element_type=jnp.float32,
    )
    filtered = filtered.astype(jnp.bfloat16).reshape(det_total, spans_here * samples)
    whitened = jnp.dot(matrix, filtered, preferred_element_type=jnp.float32).astype(jnp.bfloat16)
    smoothed = lax.dot_general(
        whitened.reshape(det_total * spans_here, samples),
        band_filter,
        (((1,), (1,)), ((), ())),
        preferred_element_type=jnp.float32,
    )
    smoothed = smoothed.astype(jnp.bfloat16).reshape(det_total, spans_here, samples)
    stokes = jnp.einsum(
        "jd,dct->cjt",
        response,
        smoothed.astype(jnp.float32) * column_weights,
        precision=precise_mode,
    )
    stokes_short = stokes.astype(jnp.bfloat16)
    partial_value = jnp.einsum(
        "cjt,cktp->ckjp", stokes_short, pointing, preferred_element_type=jnp.float32
    )
    partial_value = partial_value.reshape(row_count, comp_count * pixel_count)
    outgoing = jnp.dot(placing.astype(jnp.float32).T, partial_value, precision=precise_mode)
    outgoing = outgoing.reshape(tm_count, capacity, comp_count, pixel_count)
    arrived = lax.all_to_all(outgoing, "tm", split_axis=0, concat_axis=0, tiled=True)
    slot_hits = (
        asked_slots.reshape(-1)[None, :] == jnp.arange(tiles_own, dtype=jnp.int32)[:, None]
    ).astype(jnp.float32)
    owned_sum = jnp.dot(
        slot_hits,
        arrived.reshape(tm_count * capacity, comp_count * pixel_count),
        precision=precise_mode,
    )
    owned_sum = owned_sum.reshape(tiles_own, comp_count, pixel_count)
    summed = lax.psum(owned_sum, "wafer")
    residual_next = summed * float(det_total) ** (-0.5)
    direction_next = residual_next + blend_weight * direction
    return (updated, residual_next, direction_next)


def solution(mesh):
    in_specs = (
        P("wafer", "tm"),
        P("wafer", "tm"),
        P(),
        P(),
        P(None, ("tm", "wafer"), None),
        P(),
        P(("tm", "wafer"), None, None, None),
        P(("tm", "wafer"), None),
        P(),
        P("tm", None, None),
        P("tm", None, None),
        P(),
    )
    out_specs = (P("tm", None, None), P("tm", None, None), P("tm", None, None))
    return jax.shard_map(shards, mesh=mesh, in_specs=in_specs, out_specs=out_specs, check_vma=False)
```

profile of v0, /device:TPU:2, one launch (start us, length us, event | category | flops | bytes accessed | tf_op | source)
XLA Modules:
  0.0 281.9 jit_solution(5731134282750877064)
XLA Ops:
  12.9 12.0 %all-to-all-start = ((s32[64,1,2]{2,1,0:T(1,128)}), s32[64,1,2]{2,1,0:T(1,128)S(1)}, u32[]{:S(2)}, u32[]{:S(2)}) async-start(s32[64,1,2]{2,1,0:T(1,128)} %bitcast.2), calls=%async_computation | async-start | bytes 65536 | tf_op jit(solution)/shard_map/all_to_all | solution.py:45
  26.3 2.4 fusion.33
  28.7 4.8 %all-to-all-done = s32[64,1,2]{2,1,0:T(1,128)S(1)} async-done(((s32[64,1,2]{2,1,0:T(1,128)}), s32[64,1,2]{2,1,0:T(1,128)S(1)}, u32[]{:S(2)}, u32[]{:S(2)}) %all-to-all-start) | async-done | bytes 544 | tf_op jit(solution)/shard_map/all_to_all | solution.py:45
  35.9 5.5 %all-to-all-start.2 = ((bf16[64,2,3,256]{3,1,2,0:T(2,128)(2,1)}), bf16[64,2,3,256]{3,1,2,0:T(2,128)(2,1)S(1)}, u32[]{:S(2)}, u32[]{:S(2)}) async-start(bf16[64,2,3,256]{3,1,2,0:T(2,128)(2,1)} %broadcast_select_fusion), calls=%async_computation.2 | async-start | bytes 393216 | tf_op jit(solution)/shard_map/all_to_all | solution.py:48
  41.4 4.1 %copy.113 = bf16[256,4096]{0,1:T(8,128)(2,1)} copy(bf16[256,4096]{1,0:T(8,128)(2,1)} %param.12) | data formatting | bytes 4194304 | tf_op args[0]
  45.5 7.3 %all-to-all-done.2 = bf16[64,2,3,256]{3,1,2,0:T(2,128)(2,1)S(1)} async-done(((bf16[64,2,3,256]{3,1,2,0:T(2,128)(2,1)}), bf16[64,2,3,256]{3,1,2,0:T(2,128)(2,1)S(1)}, u32[]{:S(2)}, u32[]{:S(2)}) %all-to-all-start.2) | async-done | bytes 196640 | tf_op jit(solution)/shard_map/all_to_all | solution.py:48
  52.7 4.5 %all-to-all-start.1 = ((bf16[256,4,1024]{0,2,1:T(8,128)(2,1)}), bf16[256,4,1024]{0,2,1:T(8,128)(2,1)}, u32[]{:S(2)}, u32[]{:S(2)}) async-start(bf16[256,4,1024]{0,2,1:T(8,128)(2,1)} %bitcast.99), calls=%async_computation.1 | async-start | bytes 4194304 | tf_op jit(solution)/shard_map/all_to_all | solution.py:63
  57.2 4.1 %copy.123 = bf16[256,4096]{0,1:T(8,128)(2,1)} copy(bf16[256,4096]{1,0:T(8,128)(2,1)} %param.13) | data formatting | bytes 4194304 | tf_op args[1]
  61.3 25.7 %all-to-all-done.1 = bf16[256,4,1024]{0,2,1:T(8,128)(2,1)} async-done(((bf16[256,4,1024]{0,2,1:T(8,128)(2,1)}), bf16[256,4,1024]{0,2,1:T(8,128)(2,1)}, u32[]{:S(2)}, u32[]{:S(2)}) %all-to-all-start.1) | async-done | bytes 2097184 | tf_op jit(solution)/shard_map/all_to_all | solution.py:63
  87.1 4.6 %all-to-all-start.3 = ((bf16[256,4,1024]{0,2,1:T(8,128)(2,1)}), bf16[256,4,1024]{0,2,1:T(8,128)(2,1)}, u32[]{:S(2)}, u32[]{:S(2)}) async-start(bf16[256,4,1024]{0,2,1:T(8,128)(2,1)} %bitcast.98), calls=%async_computation.3 | async-start | bytes 4194304 | tf_op jit(solution)/shard_map/all_to_all | solution.py:64
  99.8 4.8 %copy.114 = f32[4,256,1024]{1,0,2:T(4,128)} copy(f32[4,256,1024]{1,2,0:T(8,128)S(1)} %convert_bitcast_fusion.1) | data formatting | bytes 8388608 | tf_op jit(solution)/shard_map/convert_element_type | solution.py:69
  104.7 5.8 %reshape.326 = f32[1024,4,256]{0,2,1:T(8,128)} reshape(f32[4,256,1024]{1,0,2:T(4,128)} %copy.114) | data formatting | bytes 8388608 | tf_op jit(solution)/shard_map/convert_element_type | solution.py:69
  110.5 20.1 %all-to-all-done.3 = bf16[256,4,1024]{0,2,1:T(8,128)(2,1)} async-done(((bf16[256,4,1024]{0,2,1:T(8,128)(2,1)}), bf16[256,4,1024]{0,2,1:T(8,128)(2,1)}, u32[]{:S(2)}, u32[]{:S(2)}) %all-to-all-start.3) | async-done | bytes 2097184 | tf_op jit(solution)/shard_map/all_to_all | solution.py:64
  130.6 2.2 convert_bitcast_fusion
  132.8 4.7 %copy.124 = f32[4,256,1024]{1,0,2:T(4,128)} copy(f32[4,256,1024]{1,2,0:T(8,128)S(1)} %convert_bitcast_fusion) | data formatting | bytes 8388608 | tf_op jit(solution)/shard_map/convert_element_type | solution.py:66
  137.4 5.9 %reshape.327 = f32[1024,4,256]{0,2,1:T(8,128)} reshape(f32[4,256,1024]{1,0,2:T(4,128)} %copy.124) | data formatting | bytes 8388608 | tf_op jit(solution)/shard_map/convert_element_type | solution.py:66
  143.3 7.2 %fusion.2 = bf16[1024,4,256]{0,2,1:T(8,128)(2,1)} fusion(f32[1024,4,256]{0,2,1:T(8,128)} %reshape.327, f32[1024,4,256]{0,2,1:T(8,128)} %reshape.326, f32[4,3,256]{2,1,0:T(4,128)S(1)} %convolution_bitcast_fusion, f32[3,1024]{1,0:T(4,128)S(1)} %copy-done.4), kind=kOutput, calls=%fused_computation.8 | convolution fusion | flops 40894464 | bytes 10510336 | tf_op jit(solution)/shard_map/jd,cjt->dct/dot_general | solution.py:67
  150.5 4.3 %copy.125 = bf16[1024,4,256]{2,1,0:T(4,128)(2,1)} copy(bf16[1024,4,256]{0,2,1:T(8,128)(2,1)} %fusion.2) | data formatting | bytes 4194304 | tf_op jit(solution)/shard_map/convert_element_type | solution.py:71
  154.8 4.1 %reshape.321 = bf16[4096,256]{1,0:T(8,128)(2,1)} reshape(bf16[1024,4,256]{2,1,0:T(4,128)(2,1)} %copy.125) | data formatting | bytes 4194304 | tf_op jit(solution)/shard_map/reshape | solution.py:73
  158.9 3.7 %convolution_convert_fusion.1 = bf16[4096,256]{1,0:T(8,128)(2,1)} fusion(bf16[4096,256]{1,0:T(8,128)(2,1)} %reshape.321, bf16[256,256]{1,0:T(8,128)(2,1)S(1)} %copy-done.2), kind=kOutput, calls=%fused_computation.5 | convolution fusion | flops 537919488 | bytes 4325376 | tf_op jit(solution)/shard_map/dot_general | solution.py:72
  162.5 4.4 %reshape.322 = bf16[1024,1024]{1,0:T(8,128)(2,1)} reshape(bf16[4096,256]{1,0:T(8,128)(2,1)} %convolution_convert_fusion.1) | data formatting | bytes 4194304 | tf_op jit(solution)/shard_map/reshape | solution.py:77
  166.9 7.8 %constant_dynamic-slice_fusion = bf16[1,1024,1024]{2,0,1:T(2,128)(2,1)S(1)} fusion(bf16[7,1024,1024]{2,0,1:T(8,128)(2,1)} %all-gather.2.cloned.1.call-done, s32[]{:T(128)S(6)} %select_n.167), kind=kLoop, calls=%fused_computation.81 | loop fusion | bytes 4194308 | tf_op jit(solution)/shard_map/jit(dynamic_index_in_dim)/dynamic_slice | solution.py:59
  174.7 3.7 %fusion.6 = bf16[1024,1024]{1,0:T(8,128)(2,1)} fusion(bf16[1024,1024]{1,0:T(8,128)(2,1)S(1)} %copy-done.1, bf16[1,1024,1024]{2,0,1:T(2,128)(2,1)S(1)} %constant_dynamic-slice_fusion), kind=kOutput, calls=%fused_computation.15 | convolution fusion | flops 2148532224 | bytes 6291456 | tf_op jit(solution)/shard_map/dot_general | solution.py:78
  178.4 4.4 %reshape.323 = bf16[4096,256]{1,0:T(8,128)(2,1)} reshape(bf16[1024,1024]{1,0:T(8,128)(2,1)} %fusion.6) | data formatting | bytes 4194304 | tf_op jit(solution)/shard_map/reshape | solution.py:80
  182.8 4.3 %fusion = f32[4096,256]{1,0:T(8,128)} fusion(bf16[4096,256]{1,0:T(8,128)(2,1)} %reshape.323, bf16[256,256]{1,0:T(8,128)(2,1)S(1)} %copy-done.2), kind=kOutput, calls=%fused_computation.4 | convolution fusion | flops 538968064 | bytes 6422528 | tf_op jit(solution)/shard_map/dot_general | solution.py:79
  187.1 5.2 %reshape.328 = f32[1024,4,256]{2,1,0:T(4,128)} reshape(f32[4096,256]{1,0:T(8,128)} %fusion) | data formatting | bytes 8388608 | tf_op jit(solution)/shard_map/convert_element_type | solution.py:89
  192.3 5.2 %copy.126 = f32[1024,4,256]{0,2,1:T(8,128)} copy(f32[1024,4,256]{2,1,0:T(4,128)} %reshape.328) | data formatting | bytes 8388608 | tf_op jit(solution)/shard_map/convert_element_type | solution.py:89
  197.5 7.2 %fusion.10 = bf16[4,256,3,1]{1,2,3,0:T(4,128)(2,1)S(1)} fusion(f32[1024,4,256]{0,2,1:T(8,128)} %copy.126, f32[1024,4,256]{0,2,1:T(8,128)} %reshape.327, f32[3,1024]{1,0:T(4,128)S(1)} %copy-done.4), kind=kOutput, calls=%fused_computation.18 | convolution fusion | flops 38800384 | bytes 8407040 | tf_op jit(solution)/shard_map/jd,dct->cjt/dot_general | solution.py:86
  206.7 6.5 %all-to-all-start.4 = ((f32[64,2,3,256]{3,1,2,0:T(2,128)}), f32[64,2,3,256]{3,1,2,0:T(2,128)S(1)}, u32[]{:S(2)}, u32[]{:S(2)}) async-start(f32[64,2,3,256]{3,1,2,0:T(2,128)} %copy.129), calls=%async_computation.4 | async-start | bytes 786432 | tf_op jit(solution)/shard_map/all_to_all | solution.py:99
  216.7 11.3 %all-to-all-done.4 = f32[64,2,3,256]{3,1,2,0:T(2,128)S(1)} async-done(((f32[64,2,3,256]{3,1,2,0:T(2,128)}), f32[64,2,3,256]{3,1,2,0:T(2,128)S(1)}, u32[]{:S(2)}, u32[]{:S(2)}) %all-to-all-start.4) | async-done | bytes 393248 | tf_op jit(solution)/shard_map/all_to_all | solution.py:99
  232.7 40.0 %all-reduce.2.cloned.1.call-done = f32[32,3,256]{2,0,1:T(8,128)} async-done(((f32[32,3,256]{2,0,1:T(8,128)}), f32[32,3,256]{2,0,1:T(8,128)}) %all-reduce.2.cloned.1.call-update) | async-done | bytes 98320 | tf_op jit(solution)/shard_map/psum | solution.py:109
  272.7 2.3 multiply_add_fusion
  (63 shorter events, 25.8 us)
Async XLA Ops:
  7.2 89.8 %copy-start = (bf16[4,6,256,256]{3,2,1,0:T(8,128)(2,1)S(1)}, bf16[4,6,256,256]{3,2,1,0:T(8,128)(2,1)}, u32[]{:S(2)}) copy-start(bf16[4,6,256,256]{3,2,1,0:T(8,128)(2,1)} %param.18) | copy-start | bytes 9437188
  7.2 159.8 %all-gather.2.cloned.1.call-start = ((), (), s32[]{:S(2)}) async-start(), calls=%async_computation.5 | async-start | bytes 16842752 | tf_op jit(solution)/shard_map/all_gather | solution.py:60
  12.9 20.6 %all-to-all-start = ((s32[64,1,2]{2,1,0:T(1,128)}), s32[64,1,2]{2,1,0:T(1,128)S(1)}, u32[]{:S(2)}, u32[]{:S(2)}) async-start(s32[64,1,2]{2,1,0:T(1,128)} %bitcast.2), calls=%async_computation | async-start | bytes 65536 | tf_op jit(solution)/shard_map/all_to_all | solution.py:45
  33.5 0.6 copy-start.3
  35.9 16.9 %all-to-all-start.2 = ((bf16[64,2,3,256]{3,1,2,0:T(2,128)(2,1)}), bf16[64,2,3,256]{3,1,2,0:T(2,128)(2,1)S(1)}, u32[]{:S(2)}, u32[]{:S(2)}) async-start(bf16[64,2,3,256]{3,1,2,0:T(2,128)(2,1)} %broadcast_select_fusion), calls=%async_computation.2 | async-start | bytes 393216 | tf_op jit(solution)/shard_map/all_to_all | solution.py:48
  52.7 34.3 %all-to-all-start.1 = ((bf16[256,4,1024]{0,2,1:T(8,128)(2,1)}), bf16[256,4,1024]{0,2,1:T(8,128)(2,1)}, u32[]{:S(2)}, u32[]{:S(2)}) async-start(bf16[256,4,1024]{0,2,1:T(8,128)(2,1)} %bitcast.99), calls=%async_computation.1 | async-start | bytes 4194304 | tf_op jit(solution)/shard_map/all_to_all | solution.py:63
  61.3 30.6 %copy-start.6 = (s32[64]{0:T(128)S(1)}, s32[64]{0:T(128)}, u32[]{:S(2)}) copy-start(s32[64]{0:T(128)} %param.17) | copy-start | bytes 772
  61.3 33.1 %copy-start.5 = (s32[4,6]{1,0:T(4,128)S(1)}, s32[4,6]{1,0:T(4,128)}, u32[]{:S(2)}) copy-start(s32[4,6]{1,0:T(4,128)} %param.19) | copy-start | bytes 292
  87.1 43.5 %all-to-all-start.3 = ((bf16[256,4,1024]{0,2,1:T(8,128)(2,1)}), bf16[256,4,1024]{0,2,1:T(8,128)(2,1)}, u32[]{:S(2)}, u32[]{:S(2)}) async-start(bf16[256,4,1024]{0,2,1:T(8,128)(2,1)} %bitcast.98), calls=%async_computation.3 | async-start | bytes 4194304 | tf_op jit(solution)/shard_map/all_to_all | solution.py:64
  137.4 5.9 %copy-start.4 = (f32[3,1024]{1,0:T(4,128)S(1)}, f32[3,1024]{1,0:T(4,128)}, u32[]{:S(2)}) copy-start(f32[3,1024]{1,0:T(4,128)} %param.14) | copy-start | bytes 36868
  154.8 4.1 %copy-start.2 = (bf16[256,256]{1,0:T(8,128)(2,1)S(1)}, bf16[256,256]{1,0:T(8,128)(2,1)}, u32[]{:S(2)}) copy-start(bf16[256,256]{1,0:T(8,128)(2,1)} %param.15) | copy-start | bytes 393220
  166.9 7.8 %copy-start.1 = (bf16[1024,1024]{1,0:T(8,128)(2,1)S(1)}, bf16[1024,1024]{1,0:T(8,128)(2,1)}, u32[]{:S(2)}) copy-start(bf16[1024,1024]{1,0:T(8,128)(2,1)} %reshape.322) | copy-start | bytes 6291460
  206.7 21.3 %all-to-all-start.4 = ((f32[64,2,3,256]{3,1,2,0:T(2,128)}), f32[64,2,3,256]{3,1,2,0:T(2,128)S(1)}, u32[]{:S(2)}, u32[]{:S(2)}) async-start(f32[64,2,3,256]{3,1,2,0:T(2,128)} %copy.129), calls=%async_computation.4 | async-start | bytes 786432 | tf_op jit(solution)/shard_map/all_to_all | solution.py:99
  213.2 59.5 %all-reduce.2.cloned.1.call-start = ((), (), s32[]{:S(2)}) async-start(), calls=%async_computation.6 | async-start | bytes 196608 | tf_op jit(solution)/shard_map/psum | solution.py:109
Sparse Core Ops, SparseCore 0:
  12.2 136.2 all-gather.1
  231.3 41.4 all-reduce.1
where the time goes:
time: 284 us; the launch traced here: 282 us
  waiting for transfers between devices  109 us (38%)
  local copies, waits for them, and re-layouts  82.1 us (29%)
  starting transfers between devices  33.1 us (12%)
  matrix products  28.8 us (10%)
  between operations  16.2 us (6%)
  other arithmetic  12.3 us (4%)
    psum x1, waiting for transfers between devices, shards(): summed = lax.psum(owned_sum, 'wafer')  40 us
    all_to_all x1, waiting for transfers between devices, shards(): lax.all_to_all(timestream, 'wafer', split_axis=1, concat_axis=0, tiled=True)  25.7 us
    all_to_all x1, waiting for transfers between devices, shards(): lax.all_to_all(sample_weight, 'wafer', split_axis=1, concat_axis=0, tiled...  20.1 us
    unnamed x19, local copies, waits for them, and re-layouts  12.4 us
    all_to_all x1, starting transfers between devices, shards(): lax.all_to_all(requests, 'tm', split_axis=0, concat_axis=0, tiled=True)  12 us
    all_to_all x1, waiting for transfers between devices, shards(): lax.all_to_all(outgoing, 'tm', split_axis=0, concat_axis=0, tiled=True)  11.3 us
    convert_element_type x2, local copies, waits for them, and re-layouts, shards(): columns.astype(jnp.float32).reshape(det_total, spans_here, samples) - signal  10.7 us
    convert_element_type x2, local copies, waits for them, and re-layouts, shards(): column_weights.astype(jnp.float32).reshape(det_total, spans_here, samples)  10.6 us
  transfers between devices with their start and end apart: 7, of which 6 were waited for; matrix products, arithmetic and copies ran while one was open for 27% of the time, Pallas kernels for 0%

commit v1 on v0

--- a/solution.py
+++ b/solution.py
@@ -2,6 +2,15 @@
 import jax.numpy as jnp
 from jax import lax
 from jax.sharding import PartitionSpec as P
+
+
+def draw_tables_by_axis(field):
+    w1 = jax.lax.axis_size("wafer")
+    a_next = jnp.split(field, w1, 1)
+    shaped = jnp.stack(a_next)
+    carry = jax.lax.all_to_all(shaped, "wafer", 0, 0)
+    b_now = jnp.concatenate(carry, 0)
+    return b_now
 
 
 def shards(
@@ -60,7 +69,7 @@
         lax.all_gather(whiten, ("tm", "wafer"), axis=1, tiled=True), wafer_pick, 0, keepdims=False
     )
     columns, column_weights = (
-        lax.all_to_all(timestream, "wafer", split_axis=1, concat_axis=0, tiled=True),
+        draw_tables_by_axis(timestream),
         lax.all_to_all(sample_weight, "wafer", split_axis=1, concat_axis=0, tiled=True),
     )
     column_weights = column_weights.astype(jnp.float32).reshape(det_total, spans_here, samples)

time: 284 us -> 281 us (0.989)
    all_to_all x1, waiting for transfers between devices: 20.1 us -> 26.5 us  [shards(): lax.all_to_all(sample_weight, 'wafer', split_axis=1, concat_axis=0, tiled...]
    all_to_all x1, waiting for transfers between devices: 25.7 us -> 20 us  [draw_tables_by_axis(): carry = jax.lax.all_to_all(shaped, 'wafer', 0, 0)]
    unnamed x19 -> x18, local copies, waits for them, and re-layouts: 12.4 us -> 8.28 us
  transfers between devices with their start and end apart: 7 -> 7, of which waited for: 6 -> 6; matrix products, arithmetic and copies ran while one was open for 27% -> 26% of each run, Pallas kernels for 0% -> 0%
where the time goes in v1:
time: 281 us; the launch traced here: 279 us
  waiting for transfers between devices  110 us (39%)
  local copies, waits for them, and re-layouts  79.5 us (28%)
  starting transfers between devices  33.1 us (12%)
  matrix products  28.8 us (10%)
  between operations  16.2 us (6%)
  other arithmetic  11.7 us (4%)
    psum x1, waiting for transfers between devices, shards(): summed = lax.psum(owned_sum, 'wafer')  39.8 us
    all_to_all x1, waiting for transfers between devices, shards(): lax.all_to_all(sample_weight, 'wafer', split_axis=1, concat_axis=0, tiled...  26.5 us
    all_to_all x1, waiting for transfers between devices, draw_tables_by_axis(): carry = jax.lax.all_to_all(shaped, 'wafer', 0, 0)  20 us
    all_to_all x1, starting transfers between devices, shards(): lax.all_to_all(requests, 'tm', split_axis=0, concat_axis=0, tiled=True)  12 us
    all_to_all x1, waiting for transfers between devices, shards(): lax.all_to_all(outgoing, 'tm', split_axis=0, concat_axis=0, tiled=True)  11.3 us
    convert_element_type x2, local copies, waits for them, and re-layouts, shards(): column_weights.astype(jnp.float32).reshape(det_total, spans_here, samples)  10.7 us
    convert_element_type x2, local copies, waits for them, and re-layouts, shards(): columns.astype(jnp.float32).reshape(det_total, spans_here, samples) - signal  10.6 us
    convert_element_type x2, local copies, waits for them, and re-layouts, shards(): smoothed.astype(jnp.float32) * column_weights  10.5 us
  transfers between devices with their start and end apart: 7, of which 6 were waited for; matrix products, arithmetic and copies ran while one was open for 26% of the time, Pallas kernels for 0%

profile of v1, /device:TPU:2, one launch (start us, length us, event | category | flops | bytes accessed | tf_op | source)
XLA Modules:
  0.0 279.1 jit_solution(15924905309784217733)
XLA Ops:
  12.9 12.0 %all-to-all-start = ((s32[64,1,2]{2,1,0:T(1,128)}), s32[64,1,2]{2,1,0:T(1,128)S(1)}, u32[]{:S(2)}, u32[]{:S(2)}) async-start(s32[64,1,2]{2,1,0:T(1,128)} %bitcast.2), calls=%async_computation | async-start | bytes 65536 | tf_op jit(solution)/shard_map/all_to_all | solution.py:54
  26.2 2.4 fusion.33
  28.6 4.8 %all-to-all-done = s32[64,1,2]{2,1,0:T(1,128)S(1)} async-done(((s32[64,1,2]{2,1,0:T(1,128)}), s32[64,1,2]{2,1,0:T(1,128)S(1)}, u32[]{:S(2)}, u32[]{:S(2)}) %all-to-all-start) | async-done | bytes 544 | tf_op jit(solution)/shard_map/all_to_all | solution.py:54
  35.8 5.5 %all-to-all-start.2 = ((bf16[64,2,3,256]{3,1,2,0:T(2,128)(2,1)}), bf16[64,2,3,256]{3,1,2,0:T(2,128)(2,1)S(1)}, u32[]{:S(2)}, u32[]{:S(2)}) async-start(bf16[64,2,3,256]{3,1,2,0:T(2,128)(2,1)} %broadcast_select_fusion), calls=%async_computation.2 | async-start | bytes 393216 | tf_op jit(solution)/shard_map/all_to_all | solution.py:57
  41.4 4.1 %copy.119 = bf16[256,4096]{0,1:T(8,128)(2,1)} copy(bf16[256,4096]{1,0:T(8,128)(2,1)} %param.13) | data formatting | bytes 4194304 | tf_op args[1]
  45.4 7.3 %all-to-all-done.2 = bf16[64,2,3,256]{3,1,2,0:T(2,128)(2,1)S(1)} async-done(((bf16[64,2,3,256]{3,1,2,0:T(2,128)(2,1)}), bf16[64,2,3,256]{3,1,2,0:T(2,128)(2,1)S(1)}, u32[]{:S(2)}, u32[]{:S(2)}) %all-to-all-start.2) | async-done | bytes 196640 | tf_op jit(solution)/shard_map/all_to_all | solution.py:57
  52.8 4.4 %all-to-all-start.3 = ((bf16[256,4,1024]{0,2,1:T(8,128)(2,1)}), bf16[256,4,1024]{0,2,1:T(8,128)(2,1)}, u32[]{:S(2)}, u32[]{:S(2)}) async-start(bf16[256,4,1024]{0,2,1:T(8,128)(2,1)} %bitcast.101), calls=%async_computation.3 | async-start | bytes 4194304 | tf_op jit(solution)/shard_map/all_to_all | solution.py:73
  60.5 26.5 %all-to-all-done.3 = bf16[256,4,1024]{0,2,1:T(8,128)(2,1)} async-done(((bf16[256,4,1024]{0,2,1:T(8,128)(2,1)}), bf16[256,4,1024]{0,2,1:T(8,128)(2,1)}, u32[]{:S(2)}, u32[]{:S(2)}) %all-to-all-start.3) | async-done | bytes 2097184 | tf_op jit(solution)/shard_map/all_to_all | solution.py:73
  87.1 4.7 %all-to-all-start.1 = ((bf16[4,256,1024]{2,1,0:T(8,128)(2,1)}), bf16[4,256,1024]{2,1,0:T(8,128)(2,1)}, u32[]{:S(2)}, u32[]{:S(2)}) async-start(bf16[4,256,1024]{2,1,0:T(8,128)(2,1)} %pad_maximum_fusion), calls=%async_computation.1 | async-start | bytes 4194304 | tf_op jit(solution)/shard_map/all_to_all | solution.py:11
  97.9 2.0 convert_bitcast_fusion
  99.9 4.9 %copy.120 = f32[4,256,1024]{1,0,2:T(4,128)} copy(f32[4,256,1024]{1,2,0:T(8,128)S(1)} %convert_bitcast_fusion) | data formatting | bytes 8388608 | tf_op jit(solution)/shard_map/convert_element_type | solution.py:75
  104.8 5.8 %reshape.325 = f32[1024,4,256]{0,2,1:T(8,128)} reshape(f32[4,256,1024]{1,0,2:T(4,128)} %copy.120) | data formatting | bytes 8388608 | tf_op jit(solution)/shard_map/convert_element_type | solution.py:75
  110.6 20.0 %all-to-all-done.1 = bf16[4,256,1024]{2,1,0:T(8,128)(2,1)} async-done(((bf16[4,256,1024]{2,1,0:T(8,128)(2,1)}), bf16[4,256,1024]{2,1,0:T(8,128)(2,1)}, u32[]{:S(2)}, u32[]{:S(2)}) %all-to-all-start.1) | async-done | bytes 2097184 | tf_op jit(solution)/shard_map/all_to_all | solution.py:11
  130.6 5.3 %reshape.358 = f32[1024,4,256]{2,1,0:T(4,128)} reshape(bf16[4,256,1024]{2,1,0:T(8,128)(2,1)} %all-to-all-done.1) | data formatting | bytes 6291456 | tf_op jit(solution)/shard_map/convert_element_type | solution.py:78
  135.9 5.3 %copy.133 = f32[1024,4,256]{0,2,1:T(8,128)} copy(f32[1024,4,256]{2,1,0:T(4,128)} %reshape.358) | data formatting | bytes 8388608 | tf_op jit(solution)/shard_map/convert_element_type | solution.py:78
  141.2 7.2 %fusion.2 = bf16[1024,4,256]{0,2,1:T(8,128)(2,1)} fusion(f32[1024,4,256]{0,2,1:T(8,128)} %reshape.325, f32[1024,4,256]{0,2,1:T(8,128)} %copy.133, f32[4,3,256]{2,1,0:T(4,128)S(1)} %convolution_bitcast_fusion, f32[3,1024]{1,0:T(4,128)S(1)} %copy-done.4), kind=kOutput, calls=%fused_computation.8 | convolution fusion | flops 40894464 | bytes 10510336 | tf_op jit(solution)/shard_map/jd,cjt->dct/dot_general | solution.py:76
  148.3 4.3 %copy.121 = bf16[1024,4,256]{2,1,0:T(4,128)(2,1)} copy(bf16[1024,4,256]{0,2,1:T(8,128)(2,1)} %fusion.2) | data formatting | bytes 4194304 | tf_op jit(solution)/shard_map/convert_element_type | solution.py:80
  152.6 4.0 %reshape.319 = bf16[4096,256]{1,0:T(8,128)(2,1)} reshape(bf16[1024,4,256]{2,1,0:T(4,128)(2,1)} %copy.121) | data formatting | bytes 4194304 | tf_op jit(solution)/shard_map/reshape | solution.py:82
  156.7 3.6 %convolution_convert_fusion.1 = bf16[4096,256]{1,0:T(8,128)(2,1)} fusion(bf16[4096,256]{1,0:T(8,128)(2,1)} %reshape.319, bf16[256,256]{1,0:T(8,128)(2,1)S(1)} %copy-done.2), kind=kOutput, calls=%fused_computation.5 | convolution fusion | flops 537919488 | bytes 4325376 | tf_op jit(solution)/shard_map/dot_general | solution.py:81
  160.3 4.4 %reshape.320 = bf16[1024,1024]{1,0:T(8,128)(2,1)} reshape(bf16[4096,256]{1,0:T(8,128)(2,1)} %convolution_convert_fusion.1) | data formatting | bytes 4194304 | tf_op jit(solution)/shard_map/reshape | solution.py:86
  164.7 7.5 %constant_dynamic-slice_fusion = bf16[1,1024,1024]{2,0,1:T(2,128)(2,1)S(1)} fusion(bf16[7,1024,1024]{2,0,1:T(8,128)(2,1)} %all-gather.2.cloned.1.call-done, s32[]{:T(128)S(6)} %select_n.167), kind=kLoop, calls=%fused_computation.85 | loop fusion | bytes 4194308 | tf_op jit(solution)/shard_map/jit(dynamic_index_in_dim)/dynamic_slice | solution.py:68
  172.2 3.7 %fusion.6 = bf16[1024,1024]{1,0:T(8,128)(2,1)} fusion(bf16[1024,1024]{1,0:T(8,128)(2,1)S(1)} %copy-done.1, bf16[1,1024,1024]{2,0,1:T(2,128)(2,1)S(1)} %constant_dynamic-slice_fusion), kind=kOutput, calls=%fused_computation.15 | convolution fusion | flops 2148532224 | bytes 6291456 | tf_op jit(solution)/shard_map/dot_general | solution.py:87
  175.9 4.4 %reshape.321 = bf16[4096,256]{1,0:T(8,128)(2,1)} reshape(bf16[1024,1024]{1,0:T(8,128)(2,1)} %fusion.6) | data formatting | bytes 4194304 | tf_op jit(solution)/shard_map/reshape | solution.py:89
  180.3 4.3 %fusion = f32[4096,256]{1,0:T(8,128)} fusion(bf16[4096,256]{1,0:T(8,128)(2,1)} %reshape.321, bf16[256,256]{1,0:T(8,128)(2,1)S(1)} %copy-done.2), kind=kOutput, calls=%fused_computation.4 | convolution fusion | flops 538968064 | bytes 6422528 | tf_op jit(solution)/shard_map/dot_general | solution.py:88
  184.6 5.2 %reshape.326 = f32[1024,4,256]{2,1,0:T(4,128)} reshape(f32[4096,256]{1,0:T(8,128)} %fusion) | data formatting | bytes 8388608 | tf_op jit(solution)/shard_map/convert_element_type | solution.py:98
  189.8 5.3 %copy.122 = f32[1024,4,256]{0,2,1:T(8,128)} copy(f32[1024,4,256]{2,1,0:T(4,128)} %reshape.326) | data formatting | bytes 8388608 | tf_op jit(solution)/shard_map/convert_element_type | solution.py:98
  195.1 7.2 %fusion.10 = bf16[4,256,3,1]{1,2,3,0:T(4,128)(2,1)S(1)} fusion(f32[1024,4,256]{0,2,1:T(8,128)} %copy.122, f32[1024,4,256]{0,2,1:T(8,128)} %reshape.325, f32[3,1024]{1,0:T(4,128)S(1)} %copy-done.4), kind=kOutput, calls=%fused_computation.18 | convolution fusion | flops 38800384 | bytes 8407040 | tf_op jit(solution)/shard_map/jd,dct->cjt/dot_general | solution.py:95
  204.3 6.4 %all-to-all-start.4 = ((f32[64,2,3,256]{3,1,2,0:T(2,128)}), f32[64,2,3,256]{3,1,2,0:T(2,128)S(1)}, u32[]{:S(2)}, u32[]{:S(2)}) async-start(f32[64,2,3,256]{3,1,2,0:T(2,128)} %copy.125), calls=%async_computation.4 | async-start | bytes 786432 | tf_op jit(solution)/shard_map/all_to_all | solution.py:108
  211.3 2.1 reduce.3
  214.3 11.3 %all-to-all-done.4 = f32[64,2,3,256]{3,1,2,0:T(2,128)S(1)} async-done(((f32[64,2,3,256]{3,1,2,0:T(2,128)}), f32[64,2,3,256]{3,1,2,0:T(2,128)S(1)}, u32[]{:S(2)}, u32[]{:S(2)}) %all-to-all-start.4) | async-done | bytes 393248 | tf_op jit(solution)/shard_map/all_to_all | solution.py:108
  230.2 39.8 %all-reduce.2.cloned.1.call-done = f32[32,3,256]{2,0,1:T(8,128)} async-done(((f32[32,3,256]{2,0,1:T(8,128)}), f32[32,3,256]{2,0,1:T(8,128)}) %all-reduce.2.cloned.1.call-update) | async-done | bytes 98320 | tf_op jit(solution)/shard_map/psum | solution.py:118
  270.0 2.3 multiply_add_fusion
  (63 shorter events, 25.0 us)
Async XLA Ops:
  7.2 89.8 %copy-start = (bf16[4,6,256,256]{3,2,1,0:T(8,128)(2,1)S(1)}, bf16[4,6,256,256]{3,2,1,0:T(8,128)(2,1)}, u32[]{:S(2)}) copy-start(bf16[4,6,256,256]{3,2,1,0:T(8,128)(2,1)} %param.18) | copy-start | bytes 9437188
  7.2 157.5 %all-gather.2.cloned.1.call-start = ((), (), s32[]{:S(2)}) async-start(), calls=%async_computation.5 | async-start | bytes 16842752 | tf_op jit(solution)/shard_map/all_gather | solution.py:69
  12.9 20.6 %all-to-all-start = ((s32[64,1,2]{2,1,0:T(1,128)}), s32[64,1,2]{2,1,0:T(1,128)S(1)}, u32[]{:S(2)}, u32[]{:S(2)}) async-start(s32[64,1,2]{2,1,0:T(1,128)} %bitcast.2), calls=%async_computation | async-start | bytes 65536 | tf_op jit(solution)/shard_map/all_to_all | solution.py:54
  33.5 0.6 copy-start.3
  35.8 16.9 %all-to-all-start.2 = ((bf16[64,2,3,256]{3,1,2,0:T(2,128)(2,1)}), bf16[64,2,3,256]{3,1,2,0:T(2,128)(2,1)S(1)}, u32[]{:S(2)}, u32[]{:S(2)}) async-start(bf16[64,2,3,256]{3,1,2,0:T(2,128)(2,1)} %broadcast_select_fusion), calls=%async_computation.2 | async-start | bytes 393216 | tf_op jit(solution)/shard_map/all_to_all | solution.py:57
  52.8 34.3 %all-to-all-start.3 = ((bf16[256,4,1024]{0,2,1:T(8,128)(2,1)}), bf16[256,4,1024]{0,2,1:T(8,128)(2,1)}, u32[]{:S(2)}, u32[]{:S(2)}) async-start(bf16[256,4,1024]{0,2,1:T(8,128)(2,1)} %bitcast.101), calls=%async_computation.3 | async-start | bytes 4194304 | tf_op jit(solution)/shard_map/all_to_all | solution.py:73
  60.5 31.4 %copy-start.6 = (s32[64]{0:T(128)S(1)}, s32[64]{0:T(128)}, u32[]{:S(2)}) copy-start(s32[64]{0:T(128)} %param.17) | copy-start | bytes 772
  60.5 34.0 %copy-start.5 = (s32[4,6]{1,0:T(4,128)S(1)}, s32[4,6]{1,0:T(4,128)}, u32[]{:S(2)}) copy-start(s32[4,6]{1,0:T(4,128)} %param.19) | copy-start | bytes 292
  87.1 43.5 %all-to-all-start.1 = ((bf16[4,256,1024]{2,1,0:T(8,128)(2,1)}), bf16[4,256,1024]{2,1,0:T(8,128)(2,1)}, u32[]{:S(2)}, u32[]{:S(2)}) async-start(bf16[4,256,1024]{2,1,0:T(8,128)(2,1)} %pad_maximum_fusion), calls=%async_computation.1 | async-start | bytes 4194304 | tf_op jit(solution)/shard_map/all_to_all | solution.py:11
  135.9 5.3 %copy-start.4 = (f32[3,1024]{1,0:T(4,128)S(1)}, f32[3,1024]{1,0:T(4,128)}, u32[]{:S(2)}) copy-start(f32[3,1024]{1,0:T(4,128)} %param.14) | copy-start | bytes 36868
  152.6 4.0 %copy-start.2 = (bf16[256,256]{1,0:T(8,128)(2,1)S(1)}, bf16[256,256]{1,0:T(8,128)(2,1)}, u32[]{:S(2)}) copy-start(bf16[256,256]{1,0:T(8,128)(2,1)} %param.15) | copy-start | bytes 393220
  164.7 7.5 %copy-start.1 = (bf16[1024,1024]{1,0:T(8,128)(2,1)S(1)}, bf16[1024,1024]{1,0:T(8,128)(2,1)}, u32[]{:S(2)}) copy-start(bf16[1024,1024]{1,0:T(8,128)(2,1)} %reshape.320) | copy-start | bytes 6291460
  204.3 21.2 %all-to-all-start.4 = ((f32[64,2,3,256]{3,1,2,0:T(2,128)}), f32[64,2,3,256]{3,1,2,0:T(2,128)S(1)}, u32[]{:S(2)}, u32[]{:S(2)}) async-start(f32[64,2,3,256]{3,1,2,0:T(2,128)} %copy.125), calls=%async_computation.4 | async-start | bytes 786432 | tf_op jit(solution)/shard_map/all_to_all | solution.py:108
  210.7 59.3 %all-reduce.2.cloned.1.call-start = ((), (), s32[]{:S(2)}) async-start(), calls=%async_computation.6 | async-start | bytes 196608 | tf_op jit(solution)/shard_map/psum | solution.py:118
Sparse Core Ops, SparseCore 0:
  12.2 136.3 all-gather.1
  228.8 41.2 all-reduce.1
